TPU v7x, 512 devices: a whole 4x8x8 slice. The times are simulated.
512 devices in a mesh: sk: 32 (over x, y), lang: 16 (over z, core).
Axes of the slice: x: 4, y: 8, z: 8, core: 2. Of those that a mesh axis runs over, the one named last changes fastest.
Arguments:
- embeddings: bfloat16 [524288, 1024], P(('sk', 'lang')), may hold values from -40 to 40
- omega: bfloat16 [524288, 256], P(('sk', 'lang')), may hold values from -0.0078125 to 0.0078125
- lang_ids: int32 [524288, 1], P(('sk', 'lang')), may hold values from 0 to 11; in each aligned block of 1024 rows (0 to 1023, 1024 to 2047, ...) at most 128 rows name the same one
Outputs:
- grouped: bfloat16 [1048576, 256], P(('sk', 'lang'))
Inputs may be any that keep to these rules, and one draw needn't show every extreme that they name: `lang_ids`: among the 1024 sentences of one device no language appears more than 128 times, and some language appears exactly 128 times.
All inputs are finite; a program needn't handle non-finite values.
Results may differ from a plain program's by a relative error of at most 0.0075.
Values may be sent and summed in bfloat16 or wider, within the bound.
No kernel may reach another device: no remote copies, remote signals or barrier semaphores. Data moves between devices by JAX's collectives and lax.ppermute only.
A program may use at most 64 MiB of HBM per device.

v0:
```python
import jax
import jax.numpy as jnp
from jax import lax
from jax.experimental import pallas as pl
from jax.experimental.pallas import tpu as pltpu
from jax.sharding import Mesh
from jax.sharding import PartitionSpec as P

SKETCH = 256
LANGS = 12
CAP = 128
PANEL = 32
CORES = 2


def all_sum(term):
    core = lax.axis_index("core")
    rows = term.shape[0] // CORES
    group = lax.axis_size("sk") * lax.axis_size("z")
    pair = [(0, 1), (1, 0)]
    mine = lax.dynamic_slice_in_dim(term, core * rows, rows)
    other = lax.dynamic_slice_in_dim(term, (1 - core) * rows, rows)
    half = mine + lax.ppermute(other, "core", pair)
    pieces = half.reshape(group, -1)
    slice_sum = jnp.sum(lax.all_to_all(pieces, ("sk", "z"), 0, 0, tiled=True), axis=0, keepdims=True)
    spread = jnp.broadcast_to(slice_sum, pieces.shape)
    gathered = lax.all_to_all(spread, ("sk", "z"), 0, 0, tiled=True).reshape(half.shape)
    partner = lax.ppermute(gathered, "core", pair)
    whole = lax.dynamic_update_slice_in_dim(jnp.concatenate([gathered, gathered]), partner, (1 - core) * rows, 0)
    return whole


def eliminate_kernel(g_ref, s_ref, out_ref, a_ref):
    n = g_ref.shape[0]
    width = n + s_ref.shape[1]
    a_ref[:, :n] = g_ref[...]
    a_ref[:, n:] = s_ref[...]
    sub = lax.broadcasted_iota(jnp.int32, (PANEL, 1), 0)
    diag = lax.broadcasted_iota(jnp.int32, (PANEL, width), 1) - lax.broadcasted_iota(jnp.int32, (PANEL, width), 0)
    for k in range(0, n, PANEL):
        p = a_ref[k:k + PANEL, :]
        scale = jnp.zeros((PANEL, 1), jnp.float32)
        for j in range(PANEL):
            c = k + j
            d = p[j:j + 1, c:c + 1]
            col = jnp.where(sub > j, p[:, c:c + 1] * (1.0 / d), 0.0)
            scale = jnp.where(sub == j, 1.0 / jnp.sqrt(d), scale)
            p = p - col * p[j:j + 1, :]
        p = jnp.where(diag >= k, p * scale, 0.0)
        out_ref[k:k + PANEL, :] = p[:, n:].astype(out_ref.dtype)
        if k + PANEL < n:
            c0 = ((k + PANEL) // 128) * 128
            update = lax.dot_general(
                p[:, c0:n], p, (((0,), (0,)), ((), ())),
                precision=lax.Precision.HIGHEST, preferred_element_type=jnp.float32)
            a_ref[c0:, :] = a_ref[c0:, :] - update


def orthonormal(term):
    sketch = all_sum(term)
    gram_matrix = jnp.dot(
        sketch, sketch.T, precision=lax.Precision.HIGHEST, preferred_element_type=jnp.float32
    )
    n, m = sketch.shape
    return pl.pallas_call(
        eliminate_kernel,
        out_shape=jax.ShapeDtypeStruct((n, m), jnp.bfloat16),
        in_specs=[pl.BlockSpec(memory_space=pltpu.VMEM)] * 2,
        out_specs=pl.BlockSpec(memory_space=pltpu.VMEM),
        scratch_shapes=[pltpu.VMEM((n, n + m), jnp.float32)],
    )(gram_matrix, sketch)


def on_device(embeddings, omega, lang_ids):
    def power_step(_, carry):
        term, _ = carry
        basis = orthonormal(term)
        scores = lax.dot_general(
            embeddings, basis, (((1,), (1,)), ((), ())), preferred_element_type=jnp.float32
        ).astype(jnp.bfloat16)
        following = lax.dot_general(
            scores, embeddings, (((0,), (0,)), ((), ())), preferred_element_type=jnp.float32
        )
        return following, basis

    first_term = lax.dot_general(
        omega, embeddings, (((0,), (0,)), ((), ())), preferred_element_type=jnp.float32
    )
    start = (first_term, jnp.zeros(first_term.shape, jnp.bfloat16))
    _, second_basis = lax.fori_loop(0, 2, power_step, start)
    coords = lax.dot_general(
        embeddings, second_basis, (((1,), (1,)), ((), ())), preferred_element_type=jnp.float32
    ).astype(jnp.bfloat16)
    lang_count = lax.axis_size("z") * lax.axis_size("core")
    per_owner = (LANGS + lang_count - 1) // lang_count
    languages = lang_ids[:, 0]
    member = (languages[:, None] == jnp.arange(LANGS, dtype=jnp.int32)[None, :]).astype(jnp.int32)
    position = jnp.sum(jnp.cumsum(member, axis=0) * member, axis=1) - 1
    target = languages % lang_count * (per_owner * CAP) + languages // lang_count * CAP + position
    slots = lax.broadcasted_iota(jnp.int32, (lang_count * per_owner * CAP, 1), 0)
    chooser = (slots == target[None, :]).astype(jnp.bfloat16)
    outgoing = jnp.dot(chooser, coords, preferred_element_type=jnp.float32).astype(jnp.bfloat16)
    return lax.all_to_all(outgoing, ("z", "core"), split_axis=0, concat_axis=0, tiled=True)


def solution(mesh):
    lang = mesh.shape["lang"]
    split = Mesh(mesh.devices.reshape(mesh.shape["sk"], lang // CORES, CORES), ("sk", "z", "core"))
    spec = P(("sk", "z", "core"), None)
    return jax.shard_map(
        on_device, mesh=split, in_specs=(spec, spec, spec), out_specs=spec, check_vma=False
    )
```

profile of v0, /device:TPU:1, one launch (start us, length us, event | category | flops | bytes accessed | tf_op | source)
XLA Modules:
  0.0 264.0 jit_solution(18346462263308275444)
XLA Ops:
  0.0 0.0 copy-start
  0.0 0.7 fusion.5
  0.8 3.4 %reduce-window.6 = s32[12,8,128]{2,1,0:T(8,128)S(1)} reduce-window(s32[12,8,128]{2,1,0:T(8,128)S(1)} %fusion.5, s32[]{:T(128)} %constant.47.clone.1), window={size=1x1x128 pad=0_0x0_0x127_0}, to_apply=%region_0.1 | reduce-window | flops 1560576 | bytes 98308 | tf_op jit(solution)/shard_map/reduce-window
  4.1 0.1 slice.8
  4.2 0.1 copy.6
  4.4 0.1 copy.7
  4.5 0.1 broadcast_add_fusion
  4.6 0.7 fusion.4
  5.3 0.7 fusion.8
  6.0 0.0 copy-done
  6.0 2.3 fusion.14
  8.3 218.0 %while.12 = (s32[]{:T(128)}, f32[256,1024]{1,0:T(8,128)S(1)}, bf16[256,1024]{1,0:T(8,128)(2,1)}, bf16[1024,1024]{1,0:T(8,128)(2,1)}, s32[]{:T(128)}, /*index=5*/...) while((s32[]{:T(128)}, f32[256,1024]{1,0:T(8,128)S(1)}, ...), condition=%wide.region_5.6_spmd, body=%wide.region_3.5_spmd.sunk | while | flops 1879834112 | bytes 27005316 | solution.py:90
  8.4 8.8 %collective-permute-start = (f32[128,1024]{1,0:T(8,128)S(1)}, f32[128,1024]{1,0:T(8,128)S(1)}, u32[]{:S(2)}, u32[]{:S(2)}) collective-permute-start(f32[128,1024]{1,0:T(8,128)S(1)} %constant_dynamic-slice_fusion.2), channel_id=1, source_target_pairs={{0,1},{1,0},{2,3},{3,2},{4,5},{5,4},{6,7},{7,6},{8,9},{9,8},{10,11... | collective-permute-start | bytes 1572872 | tf_op jit(solution)/shard_map/while/body/eval_jaxpr/ppermute | solution.py:23
  17.2 1.5 collective-permute-done
  18.7 0.1 dynamic-slice_add_fusion.2
  18.8 0.6 all_to_all.24
  19.4 35.2 %all_to_all.31 = f32[256,1,512]{2,1,0:T(1,128)S(1)} all-to-all(f32[256,1,512]{2,1,0:T(1,128)S(1)} %all_to_all.24), channel_id=1, replica_groups=mesh['sk'=32,'z'=8,'core'=2] {'sk','z'}, dimensions={0} | all-to-all | bytes 1048576 | tf_op jit(solution)/shard_map/while/body/eval_jaxpr/all_to_all | solution.py:25
  54.6 0.3 reduce_sum.21
  54.9 0.3 broadcast_in_dim.10
  55.2 28.1 %all_to_all.32 = f32[256,1,512]{2,1,0:T(1,128)S(1)} all-to-all(f32[256,1,512]{2,1,0:T(1,128)S(1)} %broadcast_in_dim.10), channel_id=1, replica_groups=mesh['sk'=32,'z'=8,'core'=2] {'sk','z'}, dimensions={0} | all-to-all | bytes 1048576 | tf_op jit(solution)/shard_map/while/body/eval_jaxpr/all_to_all | solution.py:27
  83.3 1.2 reduce.3
  84.6 0.2 reshape.89
  84.7 5.4 %collective-permute-start.1 = (f32[128,1024]{1,0:T(8,128)S(1)}, f32[128,1024]{1,0:T(8,128)S(1)}, u32[]{:S(2)}, u32[]{:S(2)}) collective-permute-start(f32[128,1024]{1,0:T(8,128)S(1)} %reshape.89), channel_id=1, source_target_pairs={{0,1},{1,0},{2,3},{3,2},{4,5},{5,4},{6,7},{7,6},{8,9},{9,8},{10,11... | collective-permute-start | bytes 1572872 | tf_op jit(solution)/shard_map/while/body/eval_jaxpr/ppermute | solution.py:28
  90.2 0.1 pad_maximum_fusion.2
  90.3 1.4 collective-permute-done.1
  91.8 0.0 copy-start.1
  91.8 1.7 fusion.36.g_ref
  93.5 0.0 copy-done.1
  93.5 27.1 %eval_jaxpr.1 = bf16[256,1024]{1,0:T(8,128)(2,1)S(1)} custom-call(f32[256,256]{1,0:T(8,128)} %fusion.36.g_ref, f32[256,1024]{1,0:T(8,128)} %copy-done.1), custom_call_target="tpu_custom_call" | custom-call | tf_op jit(solution)/shard_map/while/body/eval_jaxpr/pallas_call | solution.py:65
  120.6 0.0 copy-start.2
  120.7 3.7 %fusion.37 = f32[256,1024]{1,0:T(8,128)S(1)} fusion(bf16[1024,1024]{1,0:T(8,128)(2,1)} %get-tuple-element.83, bf16[256,1024]{1,0:T(8,128)(2,1)S(1)} %eval_jaxpr.1), kind=kOutput, calls=%fused_computation.1.clone.1 | convolution fusion | flops 1074003968 | bytes 3670016 | tf_op jit(solution)/shard_map/while/body/eval_jaxpr/dot_general | solution.py:81
  124.4 0.0 copy-done.2
  124.5 2.3 collective-permute-start
  126.8 1.5 collective-permute-done
  128.3 0.1 dynamic-slice_add_fusion.2
  128.4 0.6 all_to_all.24
  129.0 27.4 %all_to_all.31 = f32[256,1,512]{2,1,0:T(1,128)S(1)} all-to-all(f32[256,1,512]{2,1,0:T(1,128)S(1)} %all_to_all.24), channel_id=1, replica_groups=mesh['sk'=32,'z'=8,'core'=2] {'sk','z'}, dimensions={0} | all-to-all | bytes 1048576 | tf_op jit(solution)/shard_map/while/body/eval_jaxpr/all_to_all | solution.py:25
  156.3 0.3 reduce_sum.21
  156.7 0.3 broadcast_in_dim.10
  157.0 28.1 %all_to_all.32 = f32[256,1,512]{2,1,0:T(1,128)S(1)} all-to-all(f32[256,1,512]{2,1,0:T(1,128)S(1)} %broadcast_in_dim.10), channel_id=1, replica_groups=mesh['sk'=32,'z'=8,'core'=2] {'sk','z'}, dimensions={0} | all-to-all | bytes 1048576 | tf_op jit(solution)/shard_map/while/body/eval_jaxpr/all_to_all | solution.py:27
  185.1 1.2 reduce.3
  186.3 0.2 reshape.89
  186.5 5.4 %collective-permute-start.1 = (f32[128,1024]{1,0:T(8,128)S(1)}, f32[128,1024]{1,0:T(8,128)S(1)}, u32[]{:S(2)}, u32[]{:S(2)}) collective-permute-start(f32[128,1024]{1,0:T(8,128)S(1)} %reshape.89), channel_id=1, source_target_pairs={{0,1},{1,0},{2,3},{3,2},{4,5},{5,4},{6,7},{7,6},{8,9},{9,8},{10,11... | collective-permute-start | bytes 1572872 | tf_op jit(solution)/shard_map/while/body/eval_jaxpr/ppermute | solution.py:28
  192.0 0.1 pad_maximum_fusion.2
  192.1 1.4 collective-permute-done.1
  193.5 0.0 copy-start.1
  193.5 1.7 fusion.36.g_ref
  195.3 0.0 copy-done.1
  195.3 27.1 %eval_jaxpr.1 = bf16[256,1024]{1,0:T(8,128)(2,1)S(1)} custom-call(f32[256,256]{1,0:T(8,128)} %fusion.36.g_ref, f32[256,1024]{1,0:T(8,128)} %copy-done.1), custom_call_target="tpu_custom_call" | custom-call | tf_op jit(solution)/shard_map/while/body/eval_jaxpr/pallas_call | solution.py:65
  222.4 0.0 copy-start.2
  222.4 3.8 %fusion.37 = f32[256,1024]{1,0:T(8,128)S(1)} fusion(bf16[1024,1024]{1,0:T(8,128)(2,1)} %get-tuple-element.83, bf16[256,1024]{1,0:T(8,128)(2,1)S(1)} %eval_jaxpr.1), kind=kOutput, calls=%fused_computation.1.clone.1 | convolution fusion | flops 1074003968 | bytes 3670016 | tf_op jit(solution)/shard_map/while/body/eval_jaxpr/dot_general | solution.py:81
  226.2 0.0 copy-done.2
  226.4 4.0 %fusion.3 = bf16[2048,256]{1,0:T(8,128)(2,1)S(1)} fusion(s32[1024]{0:T(1024)S(1)} %fusion.8, bf16[256,1024]{1,0:T(8,128)(2,1)} %get-tuple-element.26, bf16[1024,1024]{1,0:T(8,128)(2,1)} %get-tuple-element.95), kind=kOutput, calls=%fused_computation.9 | convolution fusion | flops 1613496320 | bytes 3674112 | tf_op jit(solution)/shard_map/dot_general | solution.py:102
  230.4 32.7 %all_to_all.30 = bf16[16,128,256]{2,1,0:T(8,128)(2,1)S(1)} all-to-all(bf16[16,128,256]{2,1,0:T(8,128)(2,1)S(1)} %bitcast.32), channel_id=1, replica_groups=mesh['sk'=32,'z'=8,'core'=2] {'z','core'}, dimensions={0} | all-to-all | bytes 2097152 | tf_op jit(solution)/shard_map/all_to_all | solution.py:103
  263.1 1.0 copy.20
  (9 shorter events, 0.2 us)
Async XLA Ops:
  0.0 6.0 %copy-start = (bf16[1024,256]{1,0:T(8,128)(2,1)S(1)}, bf16[1024,256]{1,0:T(8,128)(2,1)}, u32[]{:S(2)}) copy-start(bf16[1024,256]{1,0:T(8,128)(2,1)} %param.6) | copy-start | bytes 1572868
  8.4 10.3 %collective-permute-start = (f32[128,1024]{1,0:T(8,128)S(1)}, f32[128,1024]{1,0:T(8,128)S(1)}, u32[]{:S(2)}, u32[]{:S(2)}) collective-permute-start(f32[128,1024]{1,0:T(8,128)S(1)} %constant_dynamic-slice_fusion.2), channel_id=1, source_target_pairs={{0,1},{1,0},{2,3},{3,2},{4,5},{5,4},{6,7},{7,6},{8,9},{9,8},{10,11... | collective-permute-start | bytes 1572872 | tf_op jit(solution)/shard_map/while/body/eval_jaxpr/ppermute | solution.py:23
  84.7 7.0 %collective-permute-start.1 = (f32[128,1024]{1,0:T(8,128)S(1)}, f32[128,1024]{1,0:T(8,128)S(1)}, u32[]{:S(2)}, u32[]{:S(2)}) collective-permute-start(f32[128,1024]{1,0:T(8,128)S(1)} %reshape.89), channel_id=1, source_target_pairs={{0,1},{1,0},{2,3},{3,2},{4,5},{5,4},{6,7},{7,6},{8,9},{9,8},{10,11... | collective-permute-start | bytes 1572872 | tf_op jit(solution)/shard_map/while/body/eval_jaxpr/ppermute | solution.py:28
  91.8 1.7 copy-start.1
  120.6 3.8 %copy-start.2 = (bf16[256,1024]{1,0:T(8,128)(2,1)}, bf16[256,1024]{1,0:T(8,128)(2,1)S(1)}, u32[]{:S(2)}) copy-start(bf16[256,1024]{1,0:T(8,128)(2,1)S(1)} %eval_jaxpr.1) | copy-start | bytes 1572868 | tf_op jit(solution)/shard_map/while
  124.5 3.8 %collective-permute-start = (f32[128,1024]{1,0:T(8,128)S(1)}, f32[128,1024]{1,0:T(8,128)S(1)}, u32[]{:S(2)}, u32[]{:S(2)}) collective-permute-start(f32[128,1024]{1,0:T(8,128)S(1)} %constant_dynamic-slice_fusion.2), channel_id=1, source_target_pairs={{0,1},{1,0},{2,3},{3,2},{4,5},{5,4},{6,7},{7,6},{8,9},{9,8},{10,11... | collective-permute-start | bytes 1572872 | tf_op jit(solution)/shard_map/while/body/eval_jaxpr/ppermute | solution.py:23
  186.5 7.0 %collective-permute-start.1 = (f32[128,1024]{1,0:T(8,128)S(1)}, f32[128,1024]{1,0:T(8,128)S(1)}, u32[]{:S(2)}, u32[]{:S(2)}) collective-permute-start(f32[128,1024]{1,0:T(8,128)S(1)} %reshape.89), channel_id=1, source_target_pairs={{0,1},{1,0},{2,3},{3,2},{4,5},{5,4},{6,7},{7,6},{8,9},{9,8},{10,11... | collective-permute-start | bytes 1572872 | tf_op jit(solution)/shard_map/while/body/eval_jaxpr/ppermute | solution.py:28
  193.5 1.7 copy-start.1
  222.4 3.8 %copy-start.2 = (bf16[256,1024]{1,0:T(8,128)(2,1)}, bf16[256,1024]{1,0:T(8,128)(2,1)S(1)}, u32[]{:S(2)}) copy-start(bf16[256,1024]{1,0:T(8,128)(2,1)S(1)} %eval_jaxpr.1) | copy-start | bytes 1572868 | tf_op jit(solution)/shard_map/while
where the time goes:
time: 265 us; the launch traced here: 264 us
  blocking collectives  151 us (57%)
  Pallas kernels  54.3 us (20%)
  starting transfers between devices  22 us (8%)
  matrix products  17.3 us (7%)
  other arithmetic  9.17 us (3%)
  waiting for transfers between devices  5.8 us (2%)
  local copies, waits for them, and re-layouts  3.62 us (1%)
    all_to_all x2, blocking collectives, all_sum(): lax.all_to_all(pieces, ('sk', 'z'), 0, 0, tiled=True)  62.5 us
    all_to_all x2, blocking collectives, all_sum(): lax.all_to_all(spread, ('sk', 'z'), 0, 0, tiled=True).reshape(half.shape)  56.2 us
    pallas_call x2, Pallas kernels, orthonormal(): pl.pallas_call(eliminate_kernel, out_shape=jax.ShapeDtypeStruct((n, m), j...  54.3 us
    all_to_all x1, blocking collectives, on_device(): lax.all_to_all(outgoing, ('z', 'core'), split_axis=0, concat_axis=0, tile...  32.7 us
    ppermute x2, starting transfers between devices, all_sum(): half = mine + lax.ppermute(other, 'core', pair)  11.1 us
    ppermute x2, starting transfers between devices, all_sum(): partner = lax.ppermute(gathered, 'core', pair)  10.9 us
    dot_general x2, matrix products, power_step(): lax.dot_general(scores, embeddings, (((0,), (0,)), ((), ())), preferred_e...  7.5 us
  transfers between devices with their start and end apart: 4, of which 4 were waited for; matrix products, arithmetic and copies ran while one was open for 0% of the time, Pallas kernels for 0%

commit v1 on v0

--- a/solution.py
+++ b/solution.py
@@ -94,8 +94,13 @@
     lang_count = lax.axis_size("z") * lax.axis_size("core")
     per_owner = (LANGS + lang_count - 1) // lang_count
     languages = lang_ids[:, 0]
-    member = (languages[:, None] == jnp.arange(LANGS, dtype=jnp.int32)[None, :]).astype(jnp.int32)
-    position = jnp.sum(jnp.cumsum(member, axis=0) * member, axis=1) - 1
+    member = (languages[:, None] == jnp.arange(LANGS, dtype=jnp.int32)[None, :]).astype(jnp.bfloat16)
+    rows = languages.shape[0]
+    earlier = (
+        lax.broadcasted_iota(jnp.int32, (rows, rows), 0) > lax.broadcasted_iota(jnp.int32, (rows, rows), 1)
+    ).astype(jnp.bfloat16)
+    counts = jnp.dot(earlier, member, preferred_element_type=jnp.float32)
+    position = jnp.sum(counts * member.astype(jnp.float32), axis=1).astype(jnp.int32)
     target = languages % lang_count * (per_owner * CAP) + languages // lang_count * CAP + position
     slots = lax.broadcasted_iota(jnp.int32, (lang_count * per_owner * CAP, 1), 0)
     chooser = (slots == target[None, :]).astype(jnp.bfloat16)

time: 265 us -> 261 us (0.985)
  other arithmetic: 9.17 us -> 4.24 us
    another operation x3 -> x0, other arithmetic: 3.48 us -> none
where the time goes in v1:
time: 261 us; the launch traced here: 260 us
  blocking collectives  151 us (58%)
  Pallas kernels  54.3 us (21%)
  starting transfers between devices  22 us (8%)
  matrix products  18.5 us (7%)
  waiting for transfers between devices  5.79 us (2%)
  other arithmetic  4.24 us (2%)
  local copies, waits for them, and re-layouts  3.3 us (1%)
    all_to_all x2, blocking collectives, all_sum(): lax.all_to_all(pieces, ('sk', 'z'), 0, 0, tiled=True)  62.5 us
    all_to_all x2, blocking collectives, all_sum(): lax.all_to_all(spread, ('sk', 'z'), 0, 0, tiled=True).reshape(half.shape)  56.2 us
    pallas_call x2, Pallas kernels, orthonormal(): pl.pallas_call(eliminate_kernel, out_shape=jax.ShapeDtypeStruct((n, m), j...  54.3 us
    all_to_all x1, blocking collectives, on_device(): lax.all_to_all(outgoing, ('z', 'core'), split_axis=0, concat_axis=0, tile...  32.7 us
    ppermute x2, starting transfers between devices, all_sum(): half = mine + lax.ppermute(other, 'core', pair)  11.1 us
    ppermute x2, starting transfers between devices, all_sum(): partner = lax.ppermute(gathered, 'core', pair)  10.9 us
    dot_general x2, matrix products, power_step(): lax.dot_general(scores, embeddings, (((0,), (0,)), ((), ())), preferred_e...  7.5 us
  transfers between devices with their start and end apart: 4, of which 4 were waited for; matrix products, arithmetic and copies ran while one was open for 0% of the time, Pallas kernels for 0%

profile of v1, /device:TPU:1, one launch (start us, length us, event | category | flops | bytes accessed | tf_op | source)
XLA Modules:
  0.0 260.0 jit_solution(18101083765581667565)
XLA Ops:
  0.0 0.0 copy-start
  0.0 1.3 fusion.6
  1.3 0.7 fusion.11
  2.0 0.0 copy-done
  2.0 2.3 fusion.17
  4.3 218.0 %while.12 = (s32[]{:T(128)}, f32[256,1024]{1,0:T(8,128)S(1)}, bf16[256,1024]{1,0:T(8,128)(2,1)}, bf16[1024,1024]{1,0:T(8,128)(2,1)}, s32[]{:T(128)}, /*index=5*/...) while((s32[]{:T(128)}, f32[256,1024]{1,0:T(8,128)S(1)}, ...), condition=%wide.region_3.0_spmd, body=%wide.region_1.3_spmd.sunk | while | flops 1879834112 | bytes 27005316 | solution.py:90
  4.4 8.8 %collective-permute-start = (f32[128,1024]{1,0:T(8,128)S(1)}, f32[128,1024]{1,0:T(8,128)S(1)}, u32[]{:S(2)}, u32[]{:S(2)}) collective-permute-start(f32[128,1024]{1,0:T(8,128)S(1)} %constant_dynamic-slice_fusion.2), channel_id=1, source_target_pairs={{0,1},{1,0},{2,3},{3,2},{4,5},{5,4},{6,7},{7,6},{8,9},{9,8},{10,11... | collective-permute-start | bytes 1572872 | tf_op jit(solution)/shard_map/while/body/eval_jaxpr/ppermute | solution.py:23
  13.2 1.5 collective-permute-done
  14.7 0.1 dynamic-slice_add_fusion.2
  14.7 0.6 all_to_all.24
  15.4 35.2 %all_to_all.31 = f32[256,1,512]{2,1,0:T(1,128)S(1)} all-to-all(f32[256,1,512]{2,1,0:T(1,128)S(1)} %all_to_all.24), channel_id=1, replica_groups=mesh['sk'=32,'z'=8,'core'=2] {'sk','z'}, dimensions={0} | all-to-all | bytes 1048576 | tf_op jit(solution)/shard_map/while/body/eval_jaxpr/all_to_all | solution.py:25
  50.5 0.3 reduce_sum.21
  50.9 0.3 broadcast_in_dim.10
  51.2 28.1 %all_to_all.32 = f32[256,1,512]{2,1,0:T(1,128)S(1)} all-to-all(f32[256,1,512]{2,1,0:T(1,128)S(1)} %broadcast_in_dim.10), channel_id=1, replica_groups=mesh['sk'=32,'z'=8,'core'=2] {'sk','z'}, dimensions={0} | all-to-all | bytes 1048576 | tf_op jit(solution)/shard_map/while/body/eval_jaxpr/all_to_all | solution.py:27
  79.3 1.2 reduce.3
  80.5 0.2 reshape.72
  80.7 5.4 %collective-permute-start.1 = (f32[128,1024]{1,0:T(8,128)S(1)}, f32[128,1024]{1,0:T(8,128)S(1)}, u32[]{:S(2)}, u32[]{:S(2)}) collective-permute-start(f32[128,1024]{1,0:T(8,128)S(1)} %reshape.72), channel_id=1, source_target_pairs={{0,1},{1,0},{2,3},{3,2},{4,5},{5,4},{6,7},{7,6},{8,9},{9,8},{10,11... | collective-permute-start | bytes 1572872 | tf_op jit(solution)/shard_map/while/body/eval_jaxpr/ppermute | solution.py:28
  86.2 0.1 pad_maximum_fusion.2
  86.3 1.4 collective-permute-done.1
  87.7 0.0 copy-start.1
  87.7 1.7 fusion.39.g_ref
  89.5 0.0 copy-done.1
  89.5 27.1 %eval_jaxpr.1 = bf16[256,1024]{1,0:T(8,128)(2,1)S(1)} custom-call(f32[256,256]{1,0:T(8,128)} %fusion.39.g_ref, f32[256,1024]{1,0:T(8,128)} %copy-done.1), custom_call_target="tpu_custom_call" | custom-call | tf_op jit(solution)/shard_map/while/body/eval_jaxpr/pallas_call | solution.py:65
  116.6 0.0 copy-start.2
  116.6 3.8 %fusion.40 = f32[256,1024]{1,0:T(8,128)S(1)} fusion(bf16[1024,1024]{1,0:T(8,128)(2,1)} %get-tuple-element.83, bf16[256,1024]{1,0:T(8,128)(2,1)S(1)} %eval_jaxpr.1), kind=kOutput, calls=%fused_computation.1.clone.1 | convolution fusion | flops 1074003968 | bytes 3670016 | tf_op jit(solution)/shard_map/while/body/eval_jaxpr/dot_general | solution.py:81
  120.4 0.0 copy-done.2
  120.5 2.3 collective-permute-start
  122.8 1.5 collective-permute-done
  124.3 0.1 dynamic-slice_add_fusion.2
  124.3 0.6 all_to_all.24
  125.0 27.3 %all_to_all.31 = f32[256,1,512]{2,1,0:T(1,128)S(1)} all-to-all(f32[256,1,512]{2,1,0:T(1,128)S(1)} %all_to_all.24), channel_id=1, replica_groups=mesh['sk'=32,'z'=8,'core'=2] {'sk','z'}, dimensions={0} | all-to-all | bytes 1048576 | tf_op jit(solution)/shard_map/while/body/eval_jaxpr/all_to_all | solution.py:25
  152.3 0.3 reduce_sum.21
  152.7 0.3 broadcast_in_dim.10
  152.9 28.1 %all_to_all.32 = f32[256,1,512]{2,1,0:T(1,128)S(1)} all-to-all(f32[256,1,512]{2,1,0:T(1,128)S(1)} %broadcast_in_dim.10), channel_id=1, replica_groups=mesh['sk'=32,'z'=8,'core'=2] {'sk','z'}, dimensions={0} | all-to-all | bytes 1048576 | tf_op jit(solution)/shard_map/while/body/eval_jaxpr/all_to_all | solution.py:27
  181.1 1.2 reduce.3
  182.3 0.2 reshape.72
  182.5 5.4 %collective-permute-start.1 = (f32[128,1024]{1,0:T(8,128)S(1)}, f32[128,1024]{1,0:T(8,128)S(1)}, u32[]{:S(2)}, u32[]{:S(2)}) collective-permute-start(f32[128,1024]{1,0:T(8,128)S(1)} %reshape.72), channel_id=1, source_target_pairs={{0,1},{1,0},{2,3},{3,2},{4,5},{5,4},{6,7},{7,6},{8,9},{9,8},{10,11... | collective-permute-start | bytes 1572872 | tf_op jit(solution)/shard_map/while/body/eval_jaxpr/ppermute | solution.py:28
  187.9 0.1 pad_maximum_fusion.2
  188.1 1.4 collective-permute-done.1
  189.5 0.0 copy-start.1
  189.5 1.7 fusion.39.g_ref
  191.2 0.0 copy-done.1
  191.2 27.1 %eval_jaxpr.1 = bf16[256,1024]{1,0:T(8,128)(2,1)S(1)} custom-call(f32[256,256]{1,0:T(8,128)} %fusion.39.g_ref, f32[256,1024]{1,0:T(8,128)} %copy-done.1), custom_call_target="tpu_custom_call" | custom-call | tf_op jit(solution)/shard_map/while/body/eval_jaxpr/pallas_call | solution.py:65
  218.4 0.0 copy-start.2
  218.4 3.7 %fusion.40 = f32[256,1024]{1,0:T(8,128)S(1)} fusion(bf16[1024,1024]{1,0:T(8,128)(2,1)} %get-tuple-element.83, bf16[256,1024]{1,0:T(8,128)(2,1)S(1)} %eval_jaxpr.1), kind=kOutput, calls=%fused_computation.1.clone.1 | convolution fusion | flops 1074003968 | bytes 3670016 | tf_op jit(solution)/shard_map/while/body/eval_jaxpr/dot_general | solution.py:81
  222.2 0.0 copy-done.2
  222.4 4.0 %fusion.4 = bf16[2048,256]{1,0:T(8,128)(2,1)S(1)} fusion(s32[1024]{0:T(1024)S(1)} %fusion.11, bf16[256,1024]{1,0:T(8,128)(2,1)} %get-tuple-element.26, bf16[1024,1024]{1,0:T(8,128)(2,1)} %get-tuple-element.95), kind=kOutput, calls=%fused_computation.11 | convolution fusion | flops 1613496320 | bytes 3674112 | tf_op jit(solution)/shard_map/dot_general | solution.py:107
  226.4 32.7 %all_to_all.30 = bf16[16,128,256]{2,1,0:T(8,128)(2,1)S(1)} all-to-all(bf16[16,128,256]{2,1,0:T(8,128)(2,1)S(1)} %bitcast.23), channel_id=1, replica_groups=mesh['sk'=32,'z'=8,'core'=2] {'z','core'}, dimensions={0} | all-to-all | bytes 2097152 | tf_op jit(solution)/shard_map/all_to_all | solution.py:108
  259.0 1.0 copy.15
  (5 shorter events, 0.2 us)
Async XLA Ops:
  0.0 2.0 copy-start
  4.4 10.3 %collective-permute-start = (f32[128,1024]{1,0:T(8,128)S(1)}, f32[128,1024]{1,0:T(8,128)S(1)}, u32[]{:S(2)}, u32[]{:S(2)}) collective-permute-start(f32[128,1024]{1,0:T(8,128)S(1)} %constant_dynamic-slice_fusion.2), channel_id=1, source_target_pairs={{0,1},{1,0},{2,3},{3,2},{4,5},{5,4},{6,7},{7,6},{8,9},{9,8},{10,11... | collective-permute-start | bytes 1572872 | tf_op jit(solution)/shard_map/while/body/eval_jaxpr/ppermute | solution.py:23
  80.7 7.0 %collective-permute-start.1 = (f32[128,1024]{1,0:T(8,128)S(1)}, f32[128,1024]{1,0:T(8,128)S(1)}, u32[]{:S(2)}, u32[]{:S(2)}) collective-permute-start(f32[128,1024]{1,0:T(8,128)S(1)} %reshape.72), channel_id=1, source_target_pairs={{0,1},{1,0},{2,3},{3,2},{4,5},{5,4},{6,7},{7,6},{8,9},{9,8},{10,11... | collective-permute-start | bytes 1572872 | tf_op jit(solution)/shard_map/while/body/eval_jaxpr/ppermute | solution.py:28
  87.7 1.7 copy-start.1
  116.6 3.8 %copy-start.2 = (bf16[256,1024]{1,0:T(8,128)(2,1)}, bf16[256,1024]{1,0:T(8,128)(2,1)S(1)}, u32[]{:S(2)}) copy-start(bf16[256,1024]{1,0:T(8,128)(2,1)S(1)} %eval_jaxpr.1) | copy-start | bytes 1572868 | tf_op jit(solution)/shard_map/while
  120.5 3.8 %collective-permute-start = (f32[128,1024]{1,0:T(8,128)S(1)}, f32[128,1024]{1,0:T(8,128)S(1)}, u32[]{:S(2)}, u32[]{:S(2)}) collective-permute-start(f32[128,1024]{1,0:T(8,128)S(1)} %constant_dynamic-slice_fusion.2), channel_id=1, source_target_pairs={{0,1},{1,0},{2,3},{3,2},{4,5},{5,4},{6,7},{7,6},{8,9},{9,8},{10,11... | collective-permute-start | bytes 1572872 | tf_op jit(solution)/shard_map/while/body/eval_jaxpr/ppermute | solution.py:23
  182.5 7.0 %collective-permute-start.1 = (f32[128,1024]{1,0:T(8,128)S(1)}, f32[128,1024]{1,0:T(8,128)S(1)}, u32[]{:S(2)}, u32[]{:S(2)}) collective-permute-start(f32[128,1024]{1,0:T(8,128)S(1)} %reshape.72), channel_id=1, source_target_pairs={{0,1},{1,0},{2,3},{3,2},{4,5},{5,4},{6,7},{7,6},{8,9},{9,8},{10,11... | collective-permute-start | bytes 1572872 | tf_op jit(solution)/shard_map/while/body/eval_jaxpr/ppermute | solution.py:28
  189.5 1.7 copy-start.1
  218.4 3.8 %copy-start.2 = (bf16[256,1024]{1,0:T(8,128)(2,1)}, bf16[256,1024]{1,0:T(8,128)(2,1)S(1)}, u32[]{:S(2)}) copy-start(bf16[256,1024]{1,0:T(8,128)(2,1)S(1)} %eval_jaxpr.1) | copy-start | bytes 1572868 | tf_op jit(solution)/shard_map/while

commit v2 on v1

--- a/solution.py
+++ b/solution.py
@@ -81,16 +81,13 @@
         following = lax.dot_general(
             scores, embeddings, (((0,), (0,)), ((), ())), preferred_element_type=jnp.float32
         )
-        return following, basis
+        return following, scores
 
     first_term = lax.dot_general(
         omega, embeddings, (((0,), (0,)), ((), ())), preferred_element_type=jnp.float32
     )
-    start = (first_term, jnp.zeros(first_term.shape, jnp.bfloat16))
-    _, second_basis = lax.fori_loop(0, 2, power_step, start)
-    coords = lax.dot_general(
-        embeddings, second_basis, (((1,), (1,)), ((), ())), preferred_element_type=jnp.float32
-    ).astype(jnp.bfloat16)
+    start = (first_term, jnp.zeros((embeddings.shape[0], SKETCH), jnp.bfloat16))
+    _, coords = lax.fori_loop(0, 2, power_step, start)
     lang_count = lax.axis_size("z") * lax.axis_size("core")
     per_owner = (LANGS + lang_count - 1) // lang_count
     languages = lang_ids[:, 0]

time: 261 us -> 260 us (level)
    dot_general x2, matrix products: 7.5 us -> 1.43 us  [power_step(): lax.dot_general(scores, embeddings, (((0,), (0,)), ((), ())), preferred_e...]
    dot_general x0 -> x2, matrix products: none -> 5.28 us  [power_step(): lax.dot_general(embeddings, basis, (((1,), (1,)), ((), ())), preferred_el...]
where the time goes in v2:
time: 260 us; the launch traced here: 259 us
  blocking collectives  151 us (58%)
  Pallas kernels  55.9 us (22%)
  starting transfers between devices  22 us (8%)
  matrix products  16.4 us (6%)
  waiting for transfers between devices  5.81 us (2%)
  other arithmetic  4.23 us (2%)
  local copies, waits for them, and re-layouts  3.44 us (1%)
    all_to_all x2, blocking collectives, all_sum(): lax.all_to_all(pieces, ('sk', 'z'), 0, 0, tiled=True)  62.5 us
    all_to_all x2, blocking collectives, all_sum(): lax.all_to_all(spread, ('sk', 'z'), 0, 0, tiled=True).reshape(half.shape)  56.3 us
    pallas_call x2, Pallas kernels, orthonormal(): pl.pallas_call(eliminate_kernel, out_shape=jax.ShapeDtypeStruct((n, m), j...  55.9 us
    all_to_all x1, blocking collectives, on_device(): lax.all_to_all(outgoing, ('z', 'core'), split_axis=0, concat_axis=0, tile...  32.7 us
    ppermute x2, starting transfers between devices, all_sum(): half = mine + lax.ppermute(other, 'core', pair)  11.1 us
    ppermute x2, starting transfers between devices, all_sum(): partner = lax.ppermute(gathered, 'core', pair)  10.9 us
    dot_general x2, matrix products, power_step(): lax.dot_general(embeddings, basis, (((1,), (1,)), ((), ())), preferred_el...  5.28 us
  transfers between devices with their start and end apart: 4, of which 4 were waited for; matrix products, arithmetic and copies ran while one was open for 0% of the time, Pallas kernels for 0%

profile of v2, /device:TPU:1, one launch (start us, length us, event | category | flops | bytes accessed | tf_op | source)
XLA Modules:
  0.0 259.5 jit_solution(6341152246816957228)
XLA Ops:
  0.0 0.0 copy-start
  0.0 1.3 fusion.5
  1.3 0.7 fusion.10
  2.0 0.0 copy-done
  2.0 2.3 fusion.17
  4.3 218.8 %while.12 = (s32[]{:T(128)}, f32[256,1024]{1,0:T(8,128)S(1)}, bf16[1024,256]{0,1:T(8,128)(2,1)}, bf16[1024,1024]{1,0:T(8,128)(2,1)}, s32[]{:T(128)}, /*index=5*/...) while((s32[]{:T(128)}, f32[256,1024]{1,0:T(8,128)S(1)}, ...), condition=%wide.region_3.0_spmd, body=%wide.region_1.3_spmd.sunk | while | flops 1879834112 | bytes 38539680 | solution.py:90
  4.4 8.8 %collective-permute-start = (f32[128,1024]{1,0:T(8,128)S(1)}, f32[128,1024]{1,0:T(8,128)S(1)}, u32[]{:S(2)}, u32[]{:S(2)}) collective-permute-start(f32[128,1024]{1,0:T(8,128)S(1)} %constant_dynamic-slice_fusion.2), channel_id=1, source_target_pairs={{0,1},{1,0},{2,3},{3,2},{4,5},{5,4},{6,7},{7,6},{8,9},{9,8},{10,11... | collective-permute-start | bytes 1572872 | tf_op jit(solution)/shard_map/while/body/eval_jaxpr/ppermute | solution.py:23
  13.2 1.5 collective-permute-done
  14.7 0.1 dynamic-slice_add_fusion.2
  14.8 0.6 all_to_all.24
  15.4 35.2 %all_to_all.31 = f32[256,1,512]{2,1,0:T(1,128)S(1)} all-to-all(f32[256,1,512]{2,1,0:T(1,128)S(1)} %all_to_all.24), channel_id=1, replica_groups=mesh['sk'=32,'z'=8,'core'=2] {'sk','z'}, dimensions={0} | all-to-all | bytes 1048576 | tf_op jit(solution)/shard_map/while/body/eval_jaxpr/all_to_all | solution.py:25
  50.6 0.3 reduce_sum.21
  50.9 0.3 broadcast_in_dim.10
  51.2 28.1 %all_to_all.32 = f32[256,1,512]{2,1,0:T(1,128)S(1)} all-to-all(f32[256,1,512]{2,1,0:T(1,128)S(1)} %broadcast_in_dim.10), channel_id=1, replica_groups=mesh['sk'=32,'z'=8,'core'=2] {'sk','z'}, dimensions={0} | all-to-all | bytes 1048576 | tf_op jit(solution)/shard_map/while/body/eval_jaxpr/all_to_all | solution.py:27
  79.3 1.2 reduce.3
  80.5 0.2 reshape.72
  80.7 5.4 %collective-permute-start.1 = (f32[128,1024]{1,0:T(8,128)S(1)}, f32[128,1024]{1,0:T(8,128)S(1)}, u32[]{:S(2)}, u32[]{:S(2)}) collective-permute-start(f32[128,1024]{1,0:T(8,128)S(1)} %reshape.72), channel_id=1, source_target_pairs={{0,1},{1,0},{2,3},{3,2},{4,5},{5,4},{6,7},{7,6},{8,9},{9,8},{10,11... | collective-permute-start | bytes 1572872 | tf_op jit(solution)/shard_map/while/body/eval_jaxpr/ppermute | solution.py:28
  86.2 0.1 pad_maximum_fusion.2
  86.3 1.4 collective-permute-done.1
  87.8 0.0 copy-start.1
  87.8 1.7 fusion.41.g_ref
  89.5 0.0 copy-done.1
  89.5 27.9 %eval_jaxpr.1 = bf16[256,1024]{1,0:T(8,128)(2,1)} custom-call(f32[256,256]{1,0:T(8,128)} %fusion.41.g_ref, f32[256,1024]{1,0:T(8,128)} %copy-done.1), custom_call_target="tpu_custom_call" | custom-call | tf_op jit(solution)/shard_map/while/body/eval_jaxpr/pallas_call | solution.py:65
  117.4 0.0 copy-start.2
  117.4 2.6 %convolution_convert_fusion.2 = bf16[256,1024]{1,0:T(8,128)(2,1)S(1)} fusion(bf16[256,1024]{1,0:T(8,128)(2,1)} %eval_jaxpr.1, bf16[1024,1024]{1,0:T(8,128)(2,1)} %get-tuple-element.83), kind=kOutput, calls=%fused_computation.clone.1 | convolution fusion | flops 537133056 | bytes 3145728 | tf_op jit(solution)/shard_map/while/body/eval_jaxpr/dot_general | solution.py:78
  120.1 0.0 copy-done.2
  120.1 0.0 copy-start.3
  120.1 0.7 fusion.42
  120.8 0.1 copy-done.3
  120.9 2.3 collective-permute-start
  123.2 1.5 collective-permute-done
  124.8 0.1 dynamic-slice_add_fusion.2
  124.8 0.6 all_to_all.24
  125.5 27.3 %all_to_all.31 = f32[256,1,512]{2,1,0:T(1,128)S(1)} all-to-all(f32[256,1,512]{2,1,0:T(1,128)S(1)} %all_to_all.24), channel_id=1, replica_groups=mesh['sk'=32,'z'=8,'core'=2] {'sk','z'}, dimensions={0} | all-to-all | bytes 1048576 | tf_op jit(solution)/shard_map/while/body/eval_jaxpr/all_to_all | solution.py:25
  152.8 0.3 reduce_sum.21
  153.1 0.3 broadcast_in_dim.10
  153.4 28.1 %all_to_all.32 = f32[256,1,512]{2,1,0:T(1,128)S(1)} all-to-all(f32[256,1,512]{2,1,0:T(1,128)S(1)} %broadcast_in_dim.10), channel_id=1, replica_groups=mesh['sk'=32,'z'=8,'core'=2] {'sk','z'}, dimensions={0} | all-to-all | bytes 1048576 | tf_op jit(solution)/shard_map/while/body/eval_jaxpr/all_to_all | solution.py:27
  181.5 1.2 reduce.3
  182.8 0.2 reshape.72
  183.0 5.4 %collective-permute-start.1 = (f32[128,1024]{1,0:T(8,128)S(1)}, f32[128,1024]{1,0:T(8,128)S(1)}, u32[]{:S(2)}, u32[]{:S(2)}) collective-permute-start(f32[128,1024]{1,0:T(8,128)S(1)} %reshape.72), channel_id=1, source_target_pairs={{0,1},{1,0},{2,3},{3,2},{4,5},{5,4},{6,7},{7,6},{8,9},{9,8},{10,11... | collective-permute-start | bytes 1572872 | tf_op jit(solution)/shard_map/while/body/eval_jaxpr/ppermute | solution.py:28
  188.4 0.1 pad_maximum_fusion.2
  188.5 1.4 collective-permute-done.1
  190.0 0.0 copy-start.1
  190.0 1.7 fusion.41.g_ref
  191.7 0.0 copy-done.1
  191.7 27.9 %eval_jaxpr.1 = bf16[256,1024]{1,0:T(8,128)(2,1)} custom-call(f32[256,256]{1,0:T(8,128)} %fusion.41.g_ref, f32[256,1024]{1,0:T(8,128)} %copy-done.1), custom_call_target="tpu_custom_call" | custom-call | tf_op jit(solution)/shard_map/while/body/eval_jaxpr/pallas_call | solution.py:65
  219.7 0.0 copy-start.2
  219.7 2.6 %convolution_convert_fusion.2 = bf16[256,1024]{1,0:T(8,128)(2,1)S(1)} fusion(bf16[256,1024]{1,0:T(8,128)(2,1)} %eval_jaxpr.1, bf16[1024,1024]{1,0:T(8,128)(2,1)} %get-tuple-element.83), kind=kOutput, calls=%fused_computation.clone.1 | convolution fusion | flops 537133056 | bytes 3145728 | tf_op jit(solution)/shard_map/while/body/eval_jaxpr/dot_general | solution.py:78
  222.3 0.0 copy-done.2
  222.3 0.0 copy-start.3
  222.3 0.7 fusion.42
  223.1 0.1 copy-done.3
  223.1 2.7 %fusion.3 = bf16[2048,256]{1,0:T(8,128)(2,1)S(1)} fusion(bf16[1024,256]{0,1:T(8,128)(2,1)} %get-tuple-element.26, s32[1024]{0:T(1024)S(1)} %fusion.10), kind=kOutput, calls=%fused_computation.10 | convolution fusion | flops 1076363264 | bytes 1576960 | tf_op jit(solution)/shard_map/dot_general | solution.py:104
  225.8 32.7 %all_to_all.30 = bf16[16,128,256]{2,1,0:T(8,128)(2,1)S(1)} all-to-all(bf16[16,128,256]{2,1,0:T(8,128)(2,1)S(1)} %bitcast.29), channel_id=1, replica_groups=mesh['sk'=32,'z'=8,'core'=2] {'z','core'}, dimensions={0} | all-to-all | bytes 2097152 | tf_op jit(solution)/shard_map/all_to_all | solution.py:105
  258.5 1.0 copy.15
  (5 shorter events, 0.2 us)
Async XLA Ops:
  0.0 2.0 copy-start
  4.4 10.3 %collective-permute-start = (f32[128,1024]{1,0:T(8,128)S(1)}, f32[128,1024]{1,0:T(8,128)S(1)}, u32[]{:S(2)}, u32[]{:S(2)}) collective-permute-start(f32[128,1024]{1,0:T(8,128)S(1)} %constant_dynamic-slice_fusion.2), channel_id=1, source_target_pairs={{0,1},{1,0},{2,3},{3,2},{4,5},{5,4},{6,7},{7,6},{8,9},{9,8},{10,11... | collective-permute-start | bytes 1572872 | tf_op jit(solution)/shard_map/while/body/eval_jaxpr/ppermute | solution.py:23
  80.7 7.0 %collective-permute-start.1 = (f32[128,1024]{1,0:T(8,128)S(1)}, f32[128,1024]{1,0:T(8,128)S(1)}, u32[]{:S(2)}, u32[]{:S(2)}) collective-permute-start(f32[128,1024]{1,0:T(8,128)S(1)} %reshape.72), channel_id=1, source_target_pairs={{0,1},{1,0},{2,3},{3,2},{4,5},{5,4},{6,7},{7,6},{8,9},{9,8},{10,11... | collective-permute-start | bytes 1572872 | tf_op jit(solution)/shard_map/while/body/eval_jaxpr/ppermute | solution.py:28
  87.8 1.7 copy-start.1
  117.4 2.6 %copy-start.2 = (bf16[1024,1024]{1,0:T(8,128)(2,1)S(1)}, bf16[1024,1024]{1,0:T(8,128)(2,1)}, u32[]{:S(2)}) copy-start(bf16[1024,1024]{1,0:T(8,128)(2,1)} %get-tuple-element.83) | copy-start | bytes 6291460 | tf_op jit(solution)/shard_map/while
  120.1 0.8 copy-start.3
  120.9 3.8 %collective-permute-start = (f32[128,1024]{1,0:T(8,128)S(1)}, f32[128,1024]{1,0:T(8,128)S(1)}, u32[]{:S(2)}, u32[]{:S(2)}) collective-permute-start(f32[128,1024]{1,0:T(8,128)S(1)} %constant_dynamic-slice_fusion.2), channel_id=1, source_target_pairs={{0,1},{1,0},{2,3},{3,2},{4,5},{5,4},{6,7},{7,6},{8,9},{9,8},{10,11... | collective-permute-start | bytes 1572872 | tf_op jit(solution)/shard_map/while/body/eval_jaxpr/ppermute | solution.py:23
  183.0 7.0 %collective-permute-start.1 = (f32[128,1024]{1,0:T(8,128)S(1)}, f32[128,1024]{1,0:T(8,128)S(1)}, u32[]{:S(2)}, u32[]{:S(2)}) collective-permute-start(f32[128,1024]{1,0:T(8,128)S(1)} %reshape.72), channel_id=1, source_target_pairs={{0,1},{1,0},{2,3},{3,2},{4,5},{5,4},{6,7},{7,6},{8,9},{9,8},{10,11... | collective-permute-start | bytes 1572872 | tf_op jit(solution)/shard_map/while/body/eval_jaxpr/ppermute | solution.py:28
  190.0 1.7 copy-start.1
  219.7 2.6 %copy-start.2 = (bf16[1024,1024]{1,0:T(8,128)(2,1)S(1)}, bf16[1024,1024]{1,0:T(8,128)(2,1)}, u32[]{:S(2)}) copy-start(bf16[1024,1024]{1,0:T(8,128)(2,1)} %get-tuple-element.83) | copy-start | bytes 6291460 | tf_op jit(solution)/shard_map/while
  222.3 0.8 copy-start.3

commit v3 on v1

--- a/solution.py
+++ b/solution.py
@@ -30,11 +30,13 @@
     return whole
 
 
-def eliminate_kernel(g_ref, s_ref, out_ref, a_ref):
-    n = g_ref.shape[0]
+def eliminate_kernel(s_ref, out_ref, a_ref):
+    n = s_ref.shape[0]
     width = n + s_ref.shape[1]
-    a_ref[:, :n] = g_ref[...]
     a_ref[:, n:] = s_ref[...]
+    a_ref[:, :n] = lax.dot_general(
+        s_ref[...], s_ref[...], (((1,), (1,)), ((), ())),
+        precision=lax.Precision.HIGHEST, preferred_element_type=jnp.float32)
     sub = lax.broadcasted_iota(jnp.int32, (PANEL, 1), 0)
     diag = lax.broadcasted_iota(jnp.int32, (PANEL, width), 1) - lax.broadcasted_iota(jnp.int32, (PANEL, width), 0)
     for k in range(0, n, PANEL):
@@ -58,17 +60,14 @@
 
 def orthonormal(term):
     sketch = all_sum(term)
-    gram_matrix = jnp.dot(
-        sketch, sketch.T, precision=lax.Precision.HIGHEST, preferred_element_type=jnp.float32
-    )
     n, m = sketch.shape
     return pl.pallas_call(
         eliminate_kernel,
         out_shape=jax.ShapeDtypeStruct((n, m), jnp.bfloat16),
-        in_specs=[pl.BlockSpec(memory_space=pltpu.VMEM)] * 2,
+        in_specs=[pl.BlockSpec(memory_space=pltpu.VMEM)],
         out_specs=pl.BlockSpec(memory_space=pltpu.VMEM),
         scratch_shapes=[pltpu.VMEM((n, n + m), jnp.float32)],
-    )(gram_matrix, sketch)
+    )(sketch)
 
 
 def on_device(embeddings, omega, lang_ids):

time: 261 us -> 262 us (level)
  matrix products: 18.5 us -> 15.1 us
  Pallas kernels: 54.3 us -> 57.5 us
    dot_general x2 -> x0, matrix products: 3.45 us -> none  [orthonormal(): jnp.dot(sketch, sketch.T, precision=lax.Precision.HIGHEST, preferred_elem...]
    pallas_call x2, Pallas kernels: 54.3 us -> 57.5 us  [orthonormal(): pl.pallas_call(eliminate_kernel, out_shape=jax.ShapeDtypeStruct((n, m), j...]
where the time goes in v3:
time: 262 us
  blocking collectives  151 us (58%)
  Pallas kernels  57.5 us (22%)
  starting transfers between devices  22 us (8%)
  matrix products  15.1 us (6%)
  waiting for transfers between devices  5.8 us (2%)
  local copies, waits for them, and re-layouts  5.22 us (2%)
  other arithmetic  4.24 us (2%)
    all_to_all x2, blocking collectives, all_sum(): lax.all_to_all(pieces, ('sk', 'z'), 0, 0, tiled=True)  62.5 us
    pallas_call x2, Pallas kernels, orthonormal(): pl.pallas_call(eliminate_kernel, out_shape=jax.ShapeDtypeStruct((n, m), j...  57.5 us
    all_to_all x2, blocking collectives, all_sum(): lax.all_to_all(spread, ('sk', 'z'), 0, 0, tiled=True).reshape(half.shape)  56.2 us
    all_to_all x1, blocking collectives, on_device(): lax.all_to_all(outgoing, ('z', 'core'), split_axis=0, concat_axis=0, tile...  32.7 us
    ppermute x2, starting transfers between devices, all_sum(): half = mine + lax.ppermute(other, 'core', pair)  11.1 us
    ppermute x2, starting transfers between devices, all_sum(): partner = lax.ppermute(gathered, 'core', pair)  10.9 us
    dot_general x2, matrix products, power_step(): lax.dot_general(scores, embeddings, (((0,), (0,)), ((), ())), preferred_e...  7.5 us
  transfers between devices with their start and end apart: 4, of which 4 were waited for; matrix products, arithmetic and copies ran while one was open for 0% of the time, Pallas kernels for 0%

profile of v3, /device:TPU:1, one launch (start us, length us, event | category | flops | bytes accessed | tf_op | source)
XLA Modules:
  0.0 261.7 jit_solution(2778916886697706891)
XLA Ops:
  0.0 0.0 copy-start
  0.0 1.3 fusion.6
  1.3 0.7 fusion.11
  2.0 0.0 copy-done
  2.0 2.3 fusion.16
  4.3 219.7 %while.12 = (s32[]{:T(128)}, f32[256,1024]{1,0:T(8,128)S(1)}, bf16[256,1024]{1,0:T(8,128)(2,1)}, bf16[1024,1024]{1,0:T(8,128)(2,1)}, s32[]{:T(128)}, /*index=5*/...) while((s32[]{:T(128)}, f32[256,1024]{1,0:T(8,128)S(1)}, ...), condition=%wide.region_3.0_spmd, body=%wide.region_1.3_spmd.sunk | while | flops 1074527744 | bytes 25694596 | solution.py:89
  4.4 8.8 %collective-permute-start = (f32[128,1024]{1,0:T(8,128)S(1)}, f32[128,1024]{1,0:T(8,128)S(1)}, u32[]{:S(2)}, u32[]{:S(2)}) collective-permute-start(f32[128,1024]{1,0:T(8,128)S(1)} %constant_dynamic-slice_fusion.2), channel_id=1, source_target_pairs={{0,1},{1,0},{2,3},{3,2},{4,5},{5,4},{6,7},{7,6},{8,9},{9,8},{10,11... | collective-permute-start | bytes 1572872 | tf_op jit(solution)/shard_map/while/body/eval_jaxpr/ppermute | solution.py:23
  13.2 1.5 collective-permute-done
  14.7 0.1 dynamic-slice_add_fusion.2
  14.7 0.6 all_to_all.24
  15.4 35.2 %all_to_all.31 = f32[256,1,512]{2,1,0:T(1,128)S(1)} all-to-all(f32[256,1,512]{2,1,0:T(1,128)S(1)} %all_to_all.24), channel_id=1, replica_groups=mesh['sk'=32,'z'=8,'core'=2] {'sk','z'}, dimensions={0} | all-to-all | bytes 1048576 | tf_op jit(solution)/shard_map/while/body/eval_jaxpr/all_to_all | solution.py:25
  50.5 0.3 reduce_sum.21
  50.9 0.3 broadcast_in_dim.10
  51.2 28.1 %all_to_all.32 = f32[256,1,512]{2,1,0:T(1,128)S(1)} all-to-all(f32[256,1,512]{2,1,0:T(1,128)S(1)} %broadcast_in_dim.10), channel_id=1, replica_groups=mesh['sk'=32,'z'=8,'core'=2] {'sk','z'}, dimensions={0} | all-to-all | bytes 1048576 | tf_op jit(solution)/shard_map/while/body/eval_jaxpr/all_to_all | solution.py:27
  79.3 1.2 reduce.3
  80.5 0.2 reshape.72
  80.7 5.4 %collective-permute-start.1 = (f32[128,1024]{1,0:T(8,128)S(1)}, f32[128,1024]{1,0:T(8,128)S(1)}, u32[]{:S(2)}, u32[]{:S(2)}) collective-permute-start(f32[128,1024]{1,0:T(8,128)S(1)} %reshape.72), channel_id=1, source_target_pairs={{0,1},{1,0},{2,3},{3,2},{4,5},{5,4},{6,7},{7,6},{8,9},{9,8},{10,11... | collective-permute-start | bytes 1572872 | tf_op jit(solution)/shard_map/while/body/eval_jaxpr/ppermute | solution.py:28
  86.2 0.1 pad_maximum_fusion.2
  86.3 1.4 collective-permute-done.1
  87.7 0.0 copy-start.1
  87.7 1.0 copy-done.1
  88.7 28.7 %eval_jaxpr.1 = bf16[256,1024]{1,0:T(8,128)(2,1)S(1)} custom-call(f32[256,1024]{1,0:T(8,128)} %copy-done.1), custom_call_target="tpu_custom_call" | custom-call | tf_op jit(solution)/shard_map/while/body/eval_jaxpr/pallas_call | solution.py:64
  117.4 0.0 copy-start.2
  117.5 3.7 %fusion.31 = f32[256,1024]{1,0:T(8,128)S(1)} fusion(bf16[1024,1024]{1,0:T(8,128)(2,1)} %get-tuple-element.83, bf16[256,1024]{1,0:T(8,128)(2,1)S(1)} %eval_jaxpr.1), kind=kOutput, calls=%fused_computation.1.clone.1 | convolution fusion | flops 1074003968 | bytes 3670016 | tf_op jit(solution)/shard_map/while/body/eval_jaxpr/dot_general | solution.py:80
  121.2 0.0 copy-done.2
  121.3 2.3 collective-permute-start
  123.6 1.5 collective-permute-done
  125.1 0.1 dynamic-slice_add_fusion.2
  125.2 0.6 all_to_all.24
  125.8 27.3 %all_to_all.31 = f32[256,1,512]{2,1,0:T(1,128)S(1)} all-to-all(f32[256,1,512]{2,1,0:T(1,128)S(1)} %all_to_all.24), channel_id=1, replica_groups=mesh['sk'=32,'z'=8,'core'=2] {'sk','z'}, dimensions={0} | all-to-all | bytes 1048576 | tf_op jit(solution)/shard_map/while/body/eval_jaxpr/all_to_all | solution.py:25
  153.1 0.3 reduce_sum.21
  153.5 0.3 broadcast_in_dim.10
  153.8 28.1 %all_to_all.32 = f32[256,1,512]{2,1,0:T(1,128)S(1)} all-to-all(f32[256,1,512]{2,1,0:T(1,128)S(1)} %broadcast_in_dim.10), channel_id=1, replica_groups=mesh['sk'=32,'z'=8,'core'=2] {'sk','z'}, dimensions={0} | all-to-all | bytes 1048576 | tf_op jit(solution)/shard_map/while/body/eval_jaxpr/all_to_all | solution.py:27
  181.9 1.2 reduce.3
  183.1 0.2 reshape.72
  183.3 5.4 %collective-permute-start.1 = (f32[128,1024]{1,0:T(8,128)S(1)}, f32[128,1024]{1,0:T(8,128)S(1)}, u32[]{:S(2)}, u32[]{:S(2)}) collective-permute-start(f32[128,1024]{1,0:T(8,128)S(1)} %reshape.72), channel_id=1, source_target_pairs={{0,1},{1,0},{2,3},{3,2},{4,5},{5,4},{6,7},{7,6},{8,9},{9,8},{10,11... | collective-permute-start | bytes 1572872 | tf_op jit(solution)/shard_map/while/body/eval_jaxpr/ppermute | solution.py:28
  188.8 0.1 pad_maximum_fusion.2
  188.9 1.4 collective-permute-done.1
  190.3 0.0 copy-start.1
  190.3 1.0 copy-done.1
  191.3 28.7 %eval_jaxpr.1 = bf16[256,1024]{1,0:T(8,128)(2,1)S(1)} custom-call(f32[256,1024]{1,0:T(8,128)} %copy-done.1), custom_call_target="tpu_custom_call" | custom-call | tf_op jit(solution)/shard_map/while/body/eval_jaxpr/pallas_call | solution.py:64
  220.0 0.0 copy-start.2
  220.0 3.7 %fusion.31 = f32[256,1024]{1,0:T(8,128)S(1)} fusion(bf16[1024,1024]{1,0:T(8,128)(2,1)} %get-tuple-element.83, bf16[256,1024]{1,0:T(8,128)(2,1)S(1)} %eval_jaxpr.1), kind=kOutput, calls=%fused_computation.1.clone.1 | convolution fusion | flops 1074003968 | bytes 3670016 | tf_op jit(solution)/shard_map/while/body/eval_jaxpr/dot_general | solution.py:80
  223.8 0.0 copy-done.2
  224.0 4.0 %fusion.4 = bf16[2048,256]{1,0:T(8,128)(2,1)S(1)} fusion(s32[1024]{0:T(1024)S(1)} %fusion.11, bf16[256,1024]{1,0:T(8,128)(2,1)} %get-tuple-element.26, bf16[1024,1024]{1,0:T(8,128)(2,1)} %get-tuple-element.95), kind=kOutput, calls=%fused_computation.11 | convolution fusion | flops 1613496320 | bytes 3674112 | tf_op jit(solution)/shard_map/dot_general | solution.py:106
  228.0 32.7 %all_to_all.30 = bf16[16,128,256]{2,1,0:T(8,128)(2,1)S(1)} all-to-all(bf16[16,128,256]{2,1,0:T(8,128)(2,1)S(1)} %bitcast.17), channel_id=1, replica_groups=mesh['sk'=32,'z'=8,'core'=2] {'z','core'}, dimensions={0} | all-to-all | bytes 2097152 | tf_op jit(solution)/shard_map/all_to_all | solution.py:107
  260.7 1.0 copy.15
  (5 shorter events, 0.2 us)
Async XLA Ops:
  0.0 2.0 copy-start
  4.4 10.3 %collective-permute-start = (f32[128,1024]{1,0:T(8,128)S(1)}, f32[128,1024]{1,0:T(8,128)S(1)}, u32[]{:S(2)}, u32[]{:S(2)}) collective-permute-start(f32[128,1024]{1,0:T(8,128)S(1)} %constant_dynamic-slice_fusion.2), channel_id=1, source_target_pairs={{0,1},{1,0},{2,3},{3,2},{4,5},{5,4},{6,7},{7,6},{8,9},{9,8},{10,11... | collective-permute-start | bytes 1572872 | tf_op jit(solution)/shard_map/while/body/eval_jaxpr/ppermute | solution.py:23
  80.7 7.0 %collective-permute-start.1 = (f32[128,1024]{1,0:T(8,128)S(1)}, f32[128,1024]{1,0:T(8,128)S(1)}, u32[]{:S(2)}, u32[]{:S(2)}) collective-permute-start(f32[128,1024]{1,0:T(8,128)S(1)} %reshape.72), channel_id=1, source_target_pairs={{0,1},{1,0},{2,3},{3,2},{4,5},{5,4},{6,7},{7,6},{8,9},{9,8},{10,11... | collective-permute-start | bytes 1572872 | tf_op jit(solution)/shard_map/while/body/eval_jaxpr/ppermute | solution.py:28
  87.7 1.0 copy-start.1
  117.4 3.8 %copy-start.2 = (bf16[256,1024]{1,0:T(8,128)(2,1)}, bf16[256,1024]{1,0:T(8,128)(2,1)S(1)}, u32[]{:S(2)}) copy-start(bf16[256,1024]{1,0:T(8,128)(2,1)S(1)} %eval_jaxpr.1) | copy-start | bytes 1572868 | tf_op jit(solution)/shard_map/while
  121.3 3.8 %collective-permute-start = (f32[128,1024]{1,0:T(8,128)S(1)}, f32[128,1024]{1,0:T(8,128)S(1)}, u32[]{:S(2)}, u32[]{:S(2)}) collective-permute-start(f32[128,1024]{1,0:T(8,128)S(1)} %constant_dynamic-slice_fusion.2), channel_id=1, source_target_pairs={{0,1},{1,0},{2,3},{3,2},{4,5},{5,4},{6,7},{7,6},{8,9},{9,8},{10,11... | collective-permute-start | bytes 1572872 | tf_op jit(solution)/shard_map/while/body/eval_jaxpr/ppermute | solution.py:23
  183.3 7.0 %collective-permute-start.1 = (f32[128,1024]{1,0:T(8,128)S(1)}, f32[128,1024]{1,0:T(8,128)S(1)}, u32[]{:S(2)}, u32[]{:S(2)}) collective-permute-start(f32[128,1024]{1,0:T(8,128)S(1)} %reshape.72), channel_id=1, source_target_pairs={{0,1},{1,0},{2,3},{3,2},{4,5},{5,4},{6,7},{7,6},{8,9},{9,8},{10,11... | collective-permute-start | bytes 1572872 | tf_op jit(solution)/shard_map/while/body/eval_jaxpr/ppermute | solution.py:28
  190.3 1.0 copy-start.1
  220.0 3.8 %copy-start.2 = (bf16[256,1024]{1,0:T(8,128)(2,1)}, bf16[256,1024]{1,0:T(8,128)(2,1)S(1)}, u32[]{:S(2)}) copy-start(bf16[256,1024]{1,0:T(8,128)(2,1)S(1)} %eval_jaxpr.1) | copy-start | bytes 1572868 | tf_op jit(solution)/shard_map/while

commit v4 on v1

--- a/solution.py
+++ b/solution.py
@@ -13,13 +13,22 @@
 CORES = 2
 
 
-def all_sum(term):
+def term_halves(weights, embeddings):
     core = lax.axis_index("core")
-    rows = term.shape[0] // CORES
+    rows = weights.shape[1] // CORES
+    dims = (((0,), (0,)), ((), ()))
+    other = lax.dot_general(lax.dynamic_slice_in_dim(weights, (1 - core) * rows, rows, axis=1), embeddings, dims,
+                            preferred_element_type=jnp.float32)
+    mine = lax.dot_general(lax.dynamic_slice_in_dim(weights, core * rows, rows, axis=1), embeddings, dims,
+                           preferred_element_type=jnp.float32)
+    return mine, other
+
+
+def all_sum(mine, other):
+    core = lax.axis_index("core")
+    rows = mine.shape[0]
     group = lax.axis_size("sk") * lax.axis_size("z")
     pair = [(0, 1), (1, 0)]
-    mine = lax.dynamic_slice_in_dim(term, core * rows, rows)
-    other = lax.dynamic_slice_in_dim(term, (1 - core) * rows, rows)
     half = mine + lax.ppermute(other, "core", pair)
     pieces = half.reshape(group, -1)
     slice_sum = jnp.sum(lax.all_to_all(pieces, ("sk", "z"), 0, 0, tiled=True), axis=0, keepdims=True)
@@ -56,8 +65,8 @@
             a_ref[c0:, :] = a_ref[c0:, :] - update
 
 
-def orthonormal(term):
-    sketch = all_sum(term)
+def orthonormal(mine, other):
+    sketch = all_sum(mine, other)
     gram_matrix = jnp.dot(
         sketch, sketch.T, precision=lax.Precision.HIGHEST, preferred_element_type=jnp.float32
     )
@@ -73,21 +82,15 @@
 
 def on_device(embeddings, omega, lang_ids):
     def power_step(_, carry):
-        term, _ = carry
-        basis = orthonormal(term)
+        mine, other, _ = carry
+        basis = orthonormal(mine, other)
         scores = lax.dot_general(
             embeddings, basis, (((1,), (1,)), ((), ())), preferred_element_type=jnp.float32
         ).astype(jnp.bfloat16)
-        following = lax.dot_general(
-            scores, embeddings, (((0,), (0,)), ((), ())), preferred_element_type=jnp.float32
-        )
-        return following, basis
+        return term_halves(scores, embeddings) + (basis,)
 
-    first_term = lax.dot_general(
-        omega, embeddings, (((0,), (0,)), ((), ())), preferred_element_type=jnp.float32
-    )
-    start = (first_term, jnp.zeros(first_term.shape, jnp.bfloat16))
-    _, second_basis = lax.fori_loop(0, 2, power_step, start)
+    start = term_halves(omega, embeddings) + (jnp.zeros((SKETCH, embeddings.shape[1]), jnp.bfloat16),)
+    _, _, second_basis = lax.fori_loop(0, 2, power_step, start)
     coords = lax.dot_general(
         embeddings, second_basis, (((1,), (1,)), ((), ())), preferred_element_type=jnp.float32
     ).astype(jnp.bfloat16)

time: 261 us -> 263 us (level)
    dot_general x3 -> x8, matrix products: 9.83 us -> 11.9 us  [the longest x3 5.36 us: term_halves(): lax.dot_general(lax.dynamic_slice_in_dim(weights, (1 - core) * rows, rows...]
where the time goes in v4:
time: 263 us
  blocking collectives  152 us (58%)
  Pallas kernels  54.3 us (21%)
  starting transfers between devices  22 us (8%)
  matrix products  20.1 us (8%)
  waiting for transfers between devices  6.22 us (2%)
  local copies, waits for them, and re-layouts  4.46 us (2%)
  other arithmetic  3.52 us (1%)
    all_to_all x2, blocking collectives, all_sum(): lax.all_to_all(pieces, ('sk', 'z'), 0, 0, tiled=True)  62.5 us
    all_to_all x2, blocking collectives, all_sum(): lax.all_to_all(spread, ('sk', 'z'), 0, 0, tiled=True).reshape(half.shape)  56.2 us
    pallas_call x2, Pallas kernels, orthonormal(): pl.pallas_call(eliminate_kernel, out_shape=jax.ShapeDtypeStruct((n, m), j...  54.3 us
    all_to_all x1, blocking collectives, on_device(): lax.all_to_all(outgoing, ('z', 'core'), split_axis=0, concat_axis=0, tile...  32.9 us
    ppermute x2, starting transfers between devices, all_sum(): half = mine + lax.ppermute(other, 'core', pair)  11.1 us
    ppermute x2, starting transfers between devices, all_sum(): partner = lax.ppermute(gathered, 'core', pair)  10.9 us
    dot_general x3, matrix products, term_halves(): lax.dot_general(lax.dynamic_slice_in_dim(weights, (1 - core) * rows, rows...  5.36 us
  transfers between devices with their start and end apart: 4, of which 4 were waited for; matrix products, arithmetic and copies ran while one was open for 0% of the time, Pallas kernels for 0%

profile of v4, /device:TPU:1, one launch (start us, length us, event | category | flops | bytes accessed | tf_op | source)
XLA Modules:
  0.0 262.6 jit_solution(11209511876336865431)
XLA Ops:
  0.0 0.0 copy-start
  0.0 0.0 copy-start.2
  0.0 1.0 copy-done
  1.0 2.9 %fusion.12 = f32[128,1024]{1,0:T(8,128)} fusion(bf16[1024,1024]{1,0:T(8,128)(2,1)} %param.5, bf16[1024,256]{1,0:T(8,128)(2,1)S(1)} %copy-done, s32[]{:T(128)S(6)} %select_n.36), kind=kOutput, calls=%fused_computation.18 | convolution fusion | flops 268435456 | bytes 2883588 | tf_op jit(solution)/shard_map/dot_general | solution.py:20
  3.9 0.0 copy-done.2
  3.9 0.0 copy-start.4
  3.9 0.5 fusion.14
  4.4 0.2 copy-done.4
  4.6 0.5 fusion.11
  5.1 219.4 %while.14 = (s32[]{:T(128)}, f32[128,1024]{1,0:T(8,128)S(1)}, f32[128,1024]{1,0:T(8,128)}, bf16[256,1024]{1,0:T(8,128)(2,1)}, bf16[1024,1024]{1,0:T(8,128)(2,1)S...) while((s32[]{:T(128)}, f32[128,1024]{1,0:T(8,128)S(1)}, ...), condition=%wide.region_3.0_spmd, body=%wide.region_1.3_spmd.sunk | while | flops 1879834112 | bytes 39588268 | solution.py:93
  5.1 8.8 %collective-permute-start = (f32[128,1024]{1,0:T(8,128)}, f32[128,1024]{1,0:T(8,128)S(1)}, u32[]{:S(2)}, u32[]{:S(2)}) collective-permute-start(f32[128,1024]{1,0:T(8,128)} %get-tuple-element.85), channel_id=1, source_target_pairs={{0,1},{1,0},{2,3},{3,2},{4,5},{5,4},{6,7},{7,6},{8,9},{9,8},{10,11... | collective-permute-start | bytes 1572872 | tf_op jit(solution)/shard_map/while/body/eval_jaxpr/ppermute | solution.py:32
  13.9 1.7 collective-permute-done
  15.6 0.1 add.71
  15.7 0.6 all_to_all.24
  16.3 35.2 %all_to_all.31 = f32[256,1,512]{2,1,0:T(1,128)S(1)} all-to-all(f32[256,1,512]{2,1,0:T(1,128)S(1)} %all_to_all.24), channel_id=1, replica_groups=mesh['sk'=32,'z'=8,'core'=2] {'sk','z'}, dimensions={0} | all-to-all | bytes 1048576 | tf_op jit(solution)/shard_map/while/body/eval_jaxpr/all_to_all | solution.py:34
  51.5 0.3 reduce_sum.21
  51.9 0.3 broadcast_in_dim.10
  52.1 28.1 %all_to_all.32 = f32[256,1,512]{2,1,0:T(1,128)S(1)} all-to-all(f32[256,1,512]{2,1,0:T(1,128)S(1)} %broadcast_in_dim.10), channel_id=1, replica_groups=mesh['sk'=32,'z'=8,'core'=2] {'sk','z'}, dimensions={0} | all-to-all | bytes 1048576 | tf_op jit(solution)/shard_map/while/body/eval_jaxpr/all_to_all | solution.py:36
  80.3 1.2 reduce.3
  81.5 0.2 reshape.72
  81.7 5.4 %collective-permute-start.1 = (f32[128,1024]{1,0:T(8,128)S(1)}, f32[128,1024]{1,0:T(8,128)S(1)}, u32[]{:S(2)}, u32[]{:S(2)}) collective-permute-start(f32[128,1024]{1,0:T(8,128)S(1)} %reshape.72), channel_id=1, source_target_pairs={{0,1},{1,0},{2,3},{3,2},{4,5},{5,4},{6,7},{7,6},{8,9},{9,8},{10,11... | collective-permute-start | bytes 1572872 | tf_op jit(solution)/shard_map/while/body/eval_jaxpr/ppermute | solution.py:37
  87.1 0.1 pad_maximum_fusion.2
  87.3 1.4 collective-permute-done.1
  88.7 0.0 copy-start.1
  88.7 1.7 fusion.57.g_ref
  90.4 0.0 copy-done.1
  90.4 27.1 %eval_jaxpr.1 = bf16[256,1024]{1,0:T(8,128)(2,1)S(1)} custom-call(f32[256,256]{1,0:T(8,128)} %fusion.57.g_ref, f32[256,1024]{1,0:T(8,128)} %copy-done.1), custom_call_target="tpu_custom_call" | custom-call | tf_op jit(solution)/shard_map/while/body/eval_jaxpr/pallas_call | solution.py:74
  117.6 0.0 copy-start.5
  117.6 0.0 copy-start.3
  117.6 2.6 convolution_convert_fusion.3
  120.2 0.0 copy-done.5
  120.2 0.0 copy-done.3
  120.2 1.3 fusion.59
  121.4 0.4 fusion.58
  121.9 2.3 collective-permute-start
  124.2 1.7 collective-permute-done
  125.9 0.1 add.71
  126.0 0.6 all_to_all.24
  126.6 27.4 %all_to_all.31 = f32[256,1,512]{2,1,0:T(1,128)S(1)} all-to-all(f32[256,1,512]{2,1,0:T(1,128)S(1)} %all_to_all.24), channel_id=1, replica_groups=mesh['sk'=32,'z'=8,'core'=2] {'sk','z'}, dimensions={0} | all-to-all | bytes 1048576 | tf_op jit(solution)/shard_map/while/body/eval_jaxpr/all_to_all | solution.py:34
  154.0 0.3 reduce_sum.21
  154.3 0.3 broadcast_in_dim.10
  154.6 28.1 %all_to_all.32 = f32[256,1,512]{2,1,0:T(1,128)S(1)} all-to-all(f32[256,1,512]{2,1,0:T(1,128)S(1)} %broadcast_in_dim.10), channel_id=1, replica_groups=mesh['sk'=32,'z'=8,'core'=2] {'sk','z'}, dimensions={0} | all-to-all | bytes 1048576 | tf_op jit(solution)/shard_map/while/body/eval_jaxpr/all_to_all | solution.py:36
  182.7 1.2 reduce.3
  184.0 0.2 reshape.72
  184.1 5.4 %collective-permute-start.1 = (f32[128,1024]{1,0:T(8,128)S(1)}, f32[128,1024]{1,0:T(8,128)S(1)}, u32[]{:S(2)}, u32[]{:S(2)}) collective-permute-start(f32[128,1024]{1,0:T(8,128)S(1)} %reshape.72), channel_id=1, source_target_pairs={{0,1},{1,0},{2,3},{3,2},{4,5},{5,4},{6,7},{7,6},{8,9},{9,8},{10,11... | collective-permute-start | bytes 1572872 | tf_op jit(solution)/shard_map/while/body/eval_jaxpr/ppermute | solution.py:37
  189.6 0.1 pad_maximum_fusion.2
  189.7 1.4 collective-permute-done.1
  191.2 0.0 copy-start.1
  191.2 1.7 fusion.57.g_ref
  192.9 0.0 copy-done.1
  192.9 27.1 %eval_jaxpr.1 = bf16[256,1024]{1,0:T(8,128)(2,1)S(1)} custom-call(f32[256,256]{1,0:T(8,128)} %fusion.57.g_ref, f32[256,1024]{1,0:T(8,128)} %copy-done.1), custom_call_target="tpu_custom_call" | custom-call | tf_op jit(solution)/shard_map/while/body/eval_jaxpr/pallas_call | solution.py:74
  220.0 0.0 copy-start.5
  220.1 0.0 copy-start.3
  220.1 2.6 convolution_convert_fusion.3
  222.6 0.0 copy-done.5
  222.6 0.0 copy-done.3
  222.7 1.3 fusion.59
  223.9 0.4 fusion.58
  224.6 4.3 %fusion.9 = bf16[2048,256]{1,0:T(8,128)(2,1)} fusion(s32[1024]{0:T(1024)S(1)} %fusion.20, bf16[256,1024]{1,0:T(8,128)(2,1)} %get-tuple-element.110, bf16[1024,1024]{1,0:T(8,128)(2,1)S(1)} %get-tuple-element.111), kind=kOutput, calls=%fused_computation.14 | convolution fusion | flops 1613496320 | bytes 3674112 | tf_op jit(solution)/shard_map/dot_general | solution.py:110
  228.8 32.9 %all_to_all.30 = bf16[16,128,256]{2,1,0:T(8,128)(2,1)S(1)} all-to-all(bf16[16,128,256]{2,1,0:T(8,128)(2,1)} %bitcast.26), channel_id=1, replica_groups=mesh['sk'=32,'z'=8,'core'=2] {'z','core'}, dimensions={0} | all-to-all | bytes 2097152 | tf_op jit(solution)/shard_map/all_to_all | solution.py:111
  261.7 1.0 copy.18
  (4 shorter events, 0.1 us)
Async XLA Ops:
  0.0 1.0 copy-start
  0.0 3.9 %copy-start.2 = (bf16[1024,1024]{1,0:T(8,128)(2,1)S(1)}, bf16[1024,1024]{1,0:T(8,128)(2,1)}, u32[]{:S(2)}) copy-start(bf16[1024,1024]{1,0:T(8,128)(2,1)} %param.5) | copy-start | bytes 6291460
  3.9 0.7 copy-start.4
  5.1 10.5 %collective-permute-start = (f32[128,1024]{1,0:T(8,128)}, f32[128,1024]{1,0:T(8,128)S(1)}, u32[]{:S(2)}, u32[]{:S(2)}) collective-permute-start(f32[128,1024]{1,0:T(8,128)} %get-tuple-element.85), channel_id=1, source_target_pairs={{0,1},{1,0},{2,3},{3,2},{4,5},{5,4},{6,7},{7,6},{8,9},{9,8},{10,11... | collective-permute-start | bytes 1572872 | tf_op jit(solution)/shard_map/while/body/eval_jaxpr/ppermute | solution.py:32
  81.7 7.0 %collective-permute-start.1 = (f32[128,1024]{1,0:T(8,128)S(1)}, f32[128,1024]{1,0:T(8,128)S(1)}, u32[]{:S(2)}, u32[]{:S(2)}) collective-permute-start(f32[128,1024]{1,0:T(8,128)S(1)} %reshape.72), channel_id=1, source_target_pairs={{0,1},{1,0},{2,3},{3,2},{4,5},{5,4},{6,7},{7,6},{8,9},{9,8},{10,11... | collective-permute-start | bytes 1572872 | tf_op jit(solution)/shard_map/while/body/eval_jaxpr/ppermute | solution.py:37
  88.7 1.7 copy-start.1
  117.6 2.6 copy-start.5
  117.6 2.6 copy-start.3
  121.9 4.0 %collective-permute-start = (f32[128,1024]{1,0:T(8,128)}, f32[128,1024]{1,0:T(8,128)S(1)}, u32[]{:S(2)}, u32[]{:S(2)}) collective-permute-start(f32[128,1024]{1,0:T(8,128)} %get-tuple-element.85), channel_id=1, source_target_pairs={{0,1},{1,0},{2,3},{3,2},{4,5},{5,4},{6,7},{7,6},{8,9},{9,8},{10,11... | collective-permute-start | bytes 1572872 | tf_op jit(solution)/shard_map/while/body/eval_jaxpr/ppermute | solution.py:32
  184.1 7.0 %collective-permute-start.1 = (f32[128,1024]{1,0:T(8,128)S(1)}, f32[128,1024]{1,0:T(8,128)S(1)}, u32[]{:S(2)}, u32[]{:S(2)}) collective-permute-start(f32[128,1024]{1,0:T(8,128)S(1)} %reshape.72), channel_id=1, source_target_pairs={{0,1},{1,0},{2,3},{3,2},{4,5},{5,4},{6,7},{7,6},{8,9},{9,8},{10,11... | collective-permute-start | bytes 1572872 | tf_op jit(solution)/shard_map/while/body/eval_jaxpr/ppermute | solution.py:37
  191.2 1.7 copy-start.1
  220.0 2.6 copy-start.5
  220.1 2.6 copy-start.3
